TPU v7x, 256 devices: a whole 4x4x8 slice. The times are simulated.
256 devices in a mesh: embed: 8 (over x, core), hidden: 32 (over y, z).
Axes of the slice: x: 4, y: 4, z: 8, core: 2. Of those that a mesh axis runs over, the one named last changes fastest.
Arguments:
- rows_in: bfloat16 [512, 16384], P('hidden', 'embed'), may hold values from -6 to 6
- gate_weight: bfloat16 [16384, 28672], P('embed', 'hidden'), may hold values from -0.046875 to 0.046875
- up_weight: bfloat16 [16384, 28672], P('embed', 'hidden'), may hold values from -0.046875 to 0.046875
- down_weight: bfloat16 [28672, 16384], P('hidden', 'embed'), may hold values from -0.03125 to 0.03125
Outputs:
- rows_out: bfloat16 [512, 16384], P('hidden', 'embed')
All inputs are finite; a program needn't handle non-finite values.
Results may differ from a plain program's by a relative error of at most 0.0049.
Values may be sent and summed in bfloat16 or wider, within the bound.
No kernel may reach another device: no remote copies, remote signals or barrier semaphores. Data moves between devices by JAX's collectives and lax.ppermute only.
A program may use at most 64 MiB of HBM per device.

v0:
```python
import jax
import jax.numpy as jnp
from jax import lax
from jax.sharding import PartitionSpec as P


def on_device(rows_in, gate_weight, up_weight, down_weight):
    width = gate_weight.shape[1]
    piece = lax.all_gather(rows_in, "hidden", axis=0, tiled=True)
    gate_part = jnp.dot(piece, gate_weight, preferred_element_type=jnp.float32)
    up_part = jnp.dot(piece, up_weight, preferred_element_type=jnp.float32)
    partial_value = jnp.concatenate([gate_part, up_part], axis=1)
    summed = lax.psum(partial_value, "embed")
    activated = (jax.nn.silu(summed[:, :width]) * summed[:, width:]).astype(jnp.bfloat16)
    totals = lax.psum_scatter(
        jnp.dot(activated, down_weight, preferred_element_type=jnp.float32),
        "hidden",
        scatter_dimension=0,
        tiled=True,
    )
    return totals.astype(jnp.bfloat16)


def solution(mesh):
    placed = (
        P("hidden", "embed"),
        P("embed", "hidden"),
        P("embed", "hidden"),
        P("hidden", "embed"),
    )
    return jax.shard_map(
        on_device, mesh=mesh, in_specs=placed, out_specs=P("hidden", "embed"), check_vma=False
    )
```

profile of v0, /device:TPU:2, one launch (start us, length us, event | category | flops | bytes accessed | tf_op | source)
XLA Modules:
  0.0 410.9 jit_solution(4857531397653067271)
XLA Ops:
  6.5 0.0 all-gather.2.cloned.1.call-start
  6.5 0.7 all-gather.2.cloned.1.call-update
  7.3 0.0 all-reduce.2.cloned.1.call-start
  7.3 83.6 %all-gather.2.cloned.1.call-done = bf16[512,2048]{1,0:T(8,128)(2,1)} async-done(((bf16[16,2048]{1,0:T(8,128)(2,1)}), bf16[512,2048]{1,0:T(8,128)(2,1)}) %all-gather.2.cloned.1.call-update) | async-done | bytes 2097168 | tf_op jit(solution)/shard_map/all_gather | solution.py:9
  90.9 0.0 copy-start
  90.9 0.0 copy-start.1
  90.9 5.1 %fusion.6 = f32[512,896]{1,0:T(8,128)S(1)} fusion(bf16[512,2048]{1,0:T(8,128)(2,1)} %all-gather.2.cloned.1.call-done, bf16[2048,896]{1,0:T(8,128)(2,1)} %param.6), kind=kOutput, calls=%fused_computation.7 | convolution fusion | flops 1879048192 | bytes 7602176 | tf_op jit(solution)/shard_map/dot_general | solution.py:11
  96.0 0.0 copy-done
  96.0 0.0 copy-done.1
  96.0 2.3 fusion.5
  98.4 2.1 pad_maximum_fusion
  100.4 0.0 all-reduce.2.cloned.1.call-update
  100.4 0.0 reduce-scatter.2.cloned.1.call-start
  100.5 70.7 %all-reduce.2.cloned.1.call-done = f32[512,1792]{1,0:T(8,128)} async-done(((f32[512,1792]{1,0:T(8,128)}), f32[512,1792]{1,0:T(8,128)}) %all-reduce.2.cloned.1.call-update) | async-done | bytes 3670032 | tf_op jit(solution)/shard_map/psum | solution.py:13
  171.2 7.4 %fusion.1 = f32[512,2048]{1,0:T(8,128)} fusion(bf16[896,2048]{1,0:T(8,128)(2,1)} %param.7, f32[512,1792]{1,0:T(8,128)} %all-reduce.2.cloned.1.call-done), kind=kOutput, calls=%fused_computation.3 | convolution fusion | flops 1881800704 | bytes 11534336 | tf_op jit(solution)/shard_map/dot_general | solution.py:16
  178.6 0.0 reduce-scatter.2.cloned.1.call-update
  178.7 224.2 %reduce-scatter.2.cloned.1.call-done = f32[16,2048]{1,0:T(8,128)} async-done(((f32[512,2048]{1,0:T(8,128)}), f32[16,2048]{1,0:T(8,128)}) %reduce-scatter.2.cloned.1.call-update) | async-done | bytes 131088 | tf_op jit(solution)/shard_map/reduce_scatter | solution.py:15
  402.9 1.5 convert_element_type.7
Async XLA Ops:
  6.5 84.3 %all-gather.2.cloned.1.call-start = ((), (), s32[]{:S(2)}) async-start(), calls=%async_computation.1 | async-start | bytes 2162688 | tf_op jit(solution)/shard_map/all_gather | solution.py:9
  7.3 163.9 %all-reduce.2.cloned.1.call-start = ((), (), s32[]{:S(2)}) async-start(), calls=%async_computation.2 | async-start | bytes 7340032 | tf_op jit(solution)/shard_map/psum | solution.py:13
  90.9 5.2 %copy-start = (bf16[2048,896]{1,0:T(8,128)(2,1)S(1)}, bf16[2048,896]{1,0:T(8,128)(2,1)}, u32[]{:S(2)}) copy-start(bf16[2048,896]{1,0:T(8,128)(2,1)} %param.5) | copy-start | bytes 11010052
  90.9 5.2 %copy-start.1 = (bf16[512,2048]{1,0:T(8,128)(2,1)S(1)}, bf16[512,2048]{1,0:T(8,128)(2,1)}, u32[]{:S(2)}) copy-start(bf16[512,2048]{1,0:T(8,128)(2,1)} %all-gather.2.cloned.1.call-done) | copy-start | bytes 6291460
  100.4 302.4 %reduce-scatter.2.cloned.1.call-start = ((), (), s32[]{:S(2)}) async-start(), calls=%async_computation.3 | async-start | bytes 4325376 | tf_op jit(solution)/shard_map/reduce_scatter | solution.py:15
Sparse Core Ops, SparseCore 0:
  9.9 80.8 all-gather.1
  100.6 70.5 all-reduce.1
  178.8 224.0 reduce-scatter.1
where the time goes:
time: 411 us
  waiting for transfers between devices  379 us (92%)
  matrix products  14.9 us (4%)
  between operations  13.1 us (3%)
    reduce_scatter x1, waiting for transfers between devices, on_device(): lax.psum_scatter(jnp.dot(activated, down_weight, preferred_element_type=j...  224 us
    all_gather x1, waiting for transfers between devices, on_device(): piece = lax.all_gather(rows_in, 'hidden', axis=0, tiled=True)  83.6 us
    psum x1, waiting for transfers between devices, on_device(): summed = lax.psum(partial_value, 'embed')  70.7 us
  transfers between devices with their start and end apart: 3, of which 3 were waited for; matrix products, arithmetic and copies ran while one was open for 0% of the time, Pallas kernels for 0%

commit v1 on v0

--- a/solution.py
+++ b/solution.py
@@ -10,7 +10,8 @@
     gate_part = jnp.dot(piece, gate_weight, preferred_element_type=jnp.float32)
     up_part = jnp.dot(piece, up_weight, preferred_element_type=jnp.float32)
     partial_value = jnp.concatenate([gate_part, up_part], axis=1)
-    summed = lax.psum(partial_value, "embed")
+    parts = lax.all_gather(partial_value, "embed")
+    summed = jnp.sum(parts, axis=0)
     activated = (jax.nn.silu(summed[:, :width]) * summed[:, width:]).astype(jnp.bfloat16)
     totals = lax.psum_scatter(
         jnp.dot(activated, down_weight, preferred_element_type=jnp.float32),

time: 411 us -> 489 us (1.19)
  waiting for transfers between devices: 379 us -> 445 us
  other arithmetic: 3.6 us -> 16.4 us
    all_gather x0 -> x1, waiting for transfers between devices: none -> 138 us  [on_device(): parts = lax.all_gather(partial_value, 'embed')]
    psum x1 -> x0, waiting for transfers between devices: 70.7 us -> none  [on_device(): summed = lax.psum(partial_value, 'embed')]
    reduce_sum x0 -> x1, other arithmetic: none -> 12.8 us  [on_device(): summed = jnp.sum(parts, axis=0)]
where the time goes in v1:
time: 489 us
  waiting for transfers between devices  445 us (91%)
  other arithmetic  16.4 us (3%)
  matrix products  14.9 us (3%)
  between operations  13.1 us (3%)
    reduce_scatter x1, waiting for transfers between devices, on_device(): lax.psum_scatter(jnp.dot(activated, down_weight, preferred_element_type=j...  223 us
    all_gather x1, waiting for transfers between devices, on_device(): parts = lax.all_gather(partial_value, 'embed')  138 us
    all_gather x1, waiting for transfers between devices, on_device(): piece = lax.all_gather(rows_in, 'hidden', axis=0, tiled=True)  83.6 us
    reduce_sum x1, other arithmetic, on_device(): summed = jnp.sum(parts, axis=0)  12.8 us
  transfers between devices with their start and end apart: 3, of which 3 were waited for; matrix products, arithmetic and copies ran while one was open for 0% of the time, Pallas kernels for 0%

profile of v1, /device:TPU:2, one launch (start us, length us, event | category | flops | bytes accessed | tf_op | source)
XLA Modules:
  0.0 489.4 jit_solution(11444634483034582942)
XLA Ops:
  6.5 0.0 all-gather.4.cloned.1.call-start
  6.5 0.7 all-gather.4.cloned.1.call-update
  7.3 0.0 all-gather.6.cloned.1.call-start
  7.3 83.6 %all-gather.4.cloned.1.call-done = bf16[512,2048]{1,0:T(8,128)(2,1)} async-done(((bf16[16,2048]{1,0:T(8,128)(2,1)}), bf16[512,2048]{1,0:T(8,128)(2,1)}) %all-gather.4.cloned.1.call-update) | async-done | bytes 2097168 | tf_op jit(solution)/shard_map/all_gather | solution.py:9
  90.9 0.0 copy-start
  90.9 0.0 copy-start.1
  90.9 5.1 %fusion.6 = f32[512,896]{1,0:T(8,128)S(1)} fusion(bf16[512,2048]{1,0:T(8,128)(2,1)} %all-gather.4.cloned.1.call-done, bf16[2048,896]{1,0:T(8,128)(2,1)} %param.6), kind=kOutput, calls=%fused_computation.7 | convolution fusion | flops 1879048192 | bytes 7602176 | tf_op jit(solution)/shard_map/dot_general | solution.py:11
  96.0 0.0 copy-done
  96.0 0.0 copy-done.1
  96.0 2.3 fusion.5
  98.4 2.1 pad_maximum_fusion
  100.4 0.0 all-gather.6.cloned.1.call-update
  100.4 0.0 reduce-scatter.2.cloned.1.call-start
  100.5 138.0 %all-gather.6.cloned.1.call-done = f32[4096,1792]{1,0:T(8,128)} async-done(((f32[512,1792]{1,0:T(8,128)}), f32[4096,1792]{1,0:T(8,128)}) %all-gather.6.cloned.1.call-update) | async-done | bytes 29360144 | tf_op jit(solution)/shard_map/all_gather | solution.py:13
  238.5 12.8 %reduce_sum.9 = f32[512,1792]{1,0:T(8,128)} reduce(f32[8,512,1792]{2,1,0:T(8,128)} %bitcast.6, f32[]{:T(128)} %constant.1.clone.1), dimensions={0}, to_apply=%region_0.0 | reduce | flops 6422528 | bytes 33030148 | tf_op jit(solution)/shard_map/reduce_sum | solution.py:14
  251.2 7.4 %fusion.1 = f32[512,2048]{1,0:T(8,128)} fusion(bf16[896,2048]{1,0:T(8,128)(2,1)} %param.7, f32[512,1792]{1,0:T(8,128)} %reduce_sum.9), kind=kOutput, calls=%fused_computation.3 | convolution fusion | flops 1881800704 | bytes 11534336 | tf_op jit(solution)/shard_map/dot_general | solution.py:17
  258.7 0.0 reduce-scatter.2.cloned.1.call-update
  258.7 222.6 %reduce-scatter.2.cloned.1.call-done = f32[16,2048]{1,0:T(8,128)} async-done(((f32[512,2048]{1,0:T(8,128)}), f32[16,2048]{1,0:T(8,128)}) %reduce-scatter.2.cloned.1.call-update) | async-done | bytes 131088 | tf_op jit(solution)/shard_map/reduce_scatter | solution.py:16
  481.3 1.5 convert_element_type.7
Async XLA Ops:
  6.5 84.3 %all-gather.4.cloned.1.call-start = ((), (), s32[]{:S(2)}) async-start(), calls=%async_computation.1 | async-start | bytes 2162688 | tf_op jit(solution)/shard_map/all_gather | solution.py:9
  7.3 231.2 %all-gather.6.cloned.1.call-start = ((), (), s32[]{:S(2)}) async-start(), calls=%async_computation.3 | async-start | bytes 33030144 | tf_op jit(solution)/shard_map/all_gather | solution.py:13
  90.9 5.2 %copy-start = (bf16[2048,896]{1,0:T(8,128)(2,1)S(1)}, bf16[2048,896]{1,0:T(8,128)(2,1)}, u32[]{:S(2)}) copy-start(bf16[2048,896]{1,0:T(8,128)(2,1)} %param.5) | copy-start | bytes 11010052
  90.9 5.2 %copy-start.1 = (bf16[512,2048]{1,0:T(8,128)(2,1)S(1)}, bf16[512,2048]{1,0:T(8,128)(2,1)}, u32[]{:S(2)}) copy-start(bf16[512,2048]{1,0:T(8,128)(2,1)} %all-gather.4.cloned.1.call-done) | copy-start | bytes 6291460
  100.4 380.9 %reduce-scatter.2.cloned.1.call-start = ((), (), s32[]{:S(2)}) async-start(), calls=%async_computation.2 | async-start | bytes 4325376 | tf_op jit(solution)/shard_map/reduce_scatter | solution.py:16
Sparse Core Ops, SparseCore 0:
  9.9 80.8 all-gather.3
  100.6 137.8 all-gather.5
  258.8 222.4 reduce-scatter.1
